TPU v7x, 32 devices: a whole 2x2x4 slice. The times are simulated.
32 devices in a mesh: groups: 2 (over y), frames: 4 (over z), heads: 4 (over x, core).
Axes of the slice: x: 2, y: 2, z: 4, core: 2. Of those that a mesh axis runs over, the one named last changes fastest.
Arguments:
- query_heads: bfloat16 [16384, 896], P(('groups', 'frames'), 'heads'), parts along dimension 0, may hold values from -6 to 6
- key_heads: bfloat16 [16384, 896], P(('groups', 'frames'), 'heads'), parts along dimension 0, may hold values from -0.04 to 8
- value_heads: bfloat16 [16384, 896], P(('groups', 'frames'), 'heads'), parts along dimension 0, may hold values from -6 to 6
- residual: bfloat16 [16384, 2240], P(('groups', 'frames', 'heads')), parts along dimension 0, may hold values from -6 to 6
- out_proj: bfloat16 [896, 2240], P('frames'), may hold values from -0.1875 to 0.1875
- frame_gate: float32 [32, 2240], P(('groups', 'frames')), parts along dimension 0, may hold values from -4 to 4
Outputs:
- updated: bfloat16 [16384, 2240], P(('groups', 'frames', 'heads')), parts along dimension 0
There are 2 independent parts, one for each index of `groups`. A program takes and returns all parts, laid end to end along the dimension named above; an argument that names none is the same for every part. Nothing has to cross between parts.
All inputs are finite; a program needn't handle non-finite values.
Results may differ from a plain program's by a relative error of at most 0.0033.
Values may be sent and summed in bfloat16 or wider, within the bound.
No kernel may reach another device: no remote copies, remote signals or barrier semaphores. Data moves between devices by JAX's collectives and lax.ppermute only.
A program may use at most 64 MiB of HBM per device.

v0:
```python
import jax
import jax.numpy as jnp
from jax import lax
from jax.sharding import PartitionSpec as P

HD = 112
HEADS_DEV = 2
FRAME_TOK = 512
EPSILON = 1e-06


def per_device(query_heads, key_heads, value_heads, residual, out_proj, frame_gate):
    length = query_heads.shape[0]
    frames_here = length // FRAME_TOK
    block_shape = (frames_here, FRAME_TOK, HEADS_DEV, HD)
    query_pos = jnp.maximum(query_heads, 0).reshape(block_shape)
    key_pos = jnp.maximum(key_heads, 0).reshape(block_shape)
    value_frames = value_heads.reshape(block_shape)
    frame_state = jnp.einsum(
        "fthi,fthj->fhij", key_pos, value_frames, preferred_element_type=jnp.float32
    )
    frame_sum = jnp.sum(key_pos, axis=1, dtype=jnp.float32)
    own_state = jnp.sum(frame_state, axis=0)
    own_sum = jnp.sum(frame_sum, axis=0)
    position = lax.axis_index("frames")
    gathered = (
        lax.all_gather(own_state[None], "frames", axis=0, tiled=True),
        lax.all_gather(own_sum[None], "frames", axis=0, tiled=True),
    )
    pieces = gathered[0].shape[0]
    is_lower = jnp.arange(pieces, dtype=jnp.int32) < position
    state_part = jnp.sum(jnp.where(is_lower[:, None, None, None], gathered[0], 0.0), axis=0)
    sum_part = jnp.sum(jnp.where(is_lower[:, None, None], gathered[1], 0.0), axis=0)
    prefix_state = state_part[None] + jnp.cumsum(frame_state, axis=0)
    prefix_sum = sum_part[None] + jnp.cumsum(frame_sum, axis=0)
    state_round = prefix_state.astype(jnp.bfloat16)
    sum_round = prefix_sum.astype(jnp.bfloat16)
    numerator = jnp.einsum(
        "fthi,fhij->fthj", query_pos, state_round, preferred_element_type=jnp.float32
    )
    denominator = (
        jnp.einsum("fthi,fhi->fth", query_pos, sum_round, preferred_element_type=jnp.float32)
        + EPSILON
    )
    attended = (
        (numerator / denominator[..., None]).astype(jnp.bfloat16).reshape(length, HEADS_DEV * HD)
    )
    rows_here = residual.shape[0]
    head_pos = lax.axis_index("heads")
    row_frame = (head_pos * rows_here + jnp.arange(rows_here, dtype=jnp.int32)) // FRAME_TOK
    selector = (row_frame[:, None] == jnp.arange(frames_here, dtype=jnp.int32)[None, :]).astype(
        jnp.float32
    )
    gate_rows = jnp.dot(
        selector, frame_gate, precision=lax.Precision.HIGHEST, preferred_element_type=jnp.float32
    )
    token_rows = lax.all_to_all(attended, "heads", split_axis=0, concat_axis=1, tiled=True)
    projected = jnp.dot(
        token_rows,
        lax.all_gather(out_proj, "frames", axis=0, tiled=True),
        preferred_element_type=jnp.float32,
    )
    return (residual.astype(jnp.float32) + gate_rows * projected).astype(jnp.bfloat16)


def solution(mesh):
    in_specs = (
        P(("groups", "frames"), "heads"),
        P(("groups", "frames"), "heads"),
        P(("groups", "frames"), "heads"),
        P(("groups", "frames", "heads"), None),
        P("frames", None),
        P(("groups", "frames"), None),
    )
    out_specs = P(("groups", "frames", "heads"), None)
    return jax.shard_map(
        per_device, mesh=mesh, in_specs=in_specs, out_specs=out_specs, check_vma=False
    )
```

profile of v0, /device:TPU:0, one launch (start us, length us, event | category | flops | bytes accessed | tf_op | source)
XLA Modules:
  0.0 113.2 jit_solution(14616134283706953128)
XLA Ops:
  6.5 0.0 copy-start
  6.5 0.0 copy-start.1
  6.5 0.0 all-gather.3.cloned.1.call-start
  6.5 0.7 all-gather.3.cloned.1.call-update
  7.3 1.4 %convert_reduce_fusion.1 = f32[224]{0:T(256)S(1)} fusion(bf16[2048,224]{0,1:T(8,128)(2,1)} %param.7), kind=kLoop, calls=%fused_computation.6 | loop fusion | flops 1376032 | bytes 918400 | tf_op jit(solution)/shard_map/reduce_sum | solution.py:24
  8.7 0.1 broadcast_in_dim.41
  8.8 1.2 %broadcast_maximum_fusion = bf16[2048,224]{0,1:T(8,128)(2,1)S(1)} fusion(bf16[2048,224]{0,1:T(8,128)(2,1)} %param.6), kind=kLoop, calls=%fused_computation.16 | loop fusion | flops 458752 | bytes 1835008 | tf_op jit(solution)/shard_map/max | solution.py:16
  10.0 0.7 reshape.48
  10.7 3.2 %reshape.47 = bf16[4,512,2,112]{1,0,3,2:T(4,128)(2,1)} reshape(bf16[2048,224]{0,1:T(8,128)(2,1)} %param.8) | data formatting | bytes 1835008 | tf_op jit(solution)/shard_map/reshape | solution.py:18
  13.9 0.0 copy-done.1
  13.9 0.1 broadcast_maximum_fusion.1
  14.0 0.7 reshape.46
  14.7 0.4 convert_reduce_fusion
  15.1 0.4 reduce_window_sum.23
  15.5 13.3 %all_gather.10 = f32[4,2,112]{2,1,0:T(2,128)S(1)} all-gather(f32[1,2,112]{2,1,0:T(2,128)S(1)} %broadcast_in_dim.41), channel_id=1, replica_groups=mesh['groups'=2,'frames'=4,'heads'=4] {'frames'}, dimensions={0}, use_global_device_ids=true | all-gather | bytes 4480 | tf_op jit(solution)/shard_map/all_gather | solution.py:28
  28.8 0.1 select_reduce_fusion.1
  28.9 0.1 fusion.12
  29.0 0.1 copy.16
  29.1 1.8 %fusion.17 = (f32[2,112,112]{2,1,0:T(8,128)S(1)}, f32[4,2,112,112]{3,2,1,0:T(8,128)S(1)}) fusion(bf16[4,512,2,112]{1,0,3,2:T(4,128)(2,1)} %reshape.47, bf16[4,512,2,112]{1,0,3,2:T(4,128)(2,1)S(1)} %reshape.46), kind=kOutput, calls=%fused_computation.36 | convolution fusion | flops 102835712 | bytes 2336768 | tf_op jit(solution)/shard_map/fthi,fthj->fhij/dot_general | solution.py:19
  30.9 19.9 %all-gather = f32[8,112,112]{2,1,0:T(8,128)S(1)} all-gather(f32[2,112,112]{2,1,0:T(8,128)S(1)} %get-tuple-element.5), channel_id=2, replica_groups=mesh['groups'=2,'frames'=4,'heads'=4] {'frames'}, dimensions={0}, use_global_device_ids=true | all-gather | bytes 501760 | tf_op jit(solution)/shard_map/all_gather | solution.py:27
  50.8 0.1 select_reduce_fusion
  50.9 0.4 fusion.7
  51.3 0.1 fusion.3
  51.3 1.4 %fusion.2 = bf16[4,512,2,112]{1,3,2,0:T(8,128)(2,1)} fusion(bf16[4,2,112,112]{3,2,1,0:T(8,128)(2,1)S(1)} %fusion.3, f32[4,512,2]{1,2,0:T(2,128)S(1)} %fusion.13, bf16[4,512,2,112]{1,0,3,2:T(4,128)(2,1)S(1)} %reshape.48), kind=kOutput, calls=%fused_computation.4 | convolution fusion | flops 103677952 | bytes 2052096 | tf_op jit(solution)/shard_map/fthi,fhij->fthj/dot_general | solution.py:38
  52.7 0.0 copy-start.2
  52.7 3.6 %all-to-all-start = ((bf16[4,512,224]{1,2,0:T(8,128)(2,1)}), bf16[4,512,224]{1,2,0:T(8,128)(2,1)S(1)}, u32[]{:S(2)}, u32[]{:S(2)}) async-start(bf16[4,512,224]{1,2,0:T(8,128)(2,1)} %bitcast.5), calls=%async_computation | async-start | bytes 1835008 | tf_op jit(solution)/shard_map/all_to_all | solution.py:57
  56.4 0.0 copy-done
  56.4 4.1 %fusion.10 = f32[512,2240]{0,1:T(8,128)} fusion(f32[4,2240]{1,0:T(4,128)S(1)} %copy-done, s32[512]{0:T(512)S(1)} %add_select_fusion), kind=kOutput, calls=%fused_computation.19 | convolution fusion | flops 55052288 | bytes 4625408 | tf_op jit(solution)/shard_map/dot_general | solution.py:54
  60.5 8.8 %all-to-all-done = bf16[4,512,224]{1,2,0:T(8,128)(2,1)S(1)} async-done(((bf16[4,512,224]{1,2,0:T(8,128)(2,1)}), bf16[4,512,224]{1,2,0:T(8,128)(2,1)S(1)}, u32[]{:S(2)}, u32[]{:S(2)}) %all-to-all-start) | async-done | bytes 917536 | tf_op jit(solution)/shard_map/all_to_all | solution.py:57
  69.4 29.2 %all-gather.3.cloned.1.call-done = bf16[896,2240]{1,0:T(8,128)(2,1)} async-done(((bf16[224,2240]{1,0:T(8,128)(2,1)}), bf16[896,2240]{1,0:T(8,128)(2,1)}) %all-gather.3.cloned.1.call-update) | async-done | bytes 4014096 | tf_op jit(solution)/shard_map/all_gather | solution.py:60
  98.6 0.0 copy-done.2
  98.6 7.8 %fusion.1 = bf16[512,2240]{0,1:T(8,128)(2,1)} fusion(f32[512,2240]{0,1:T(8,128)} %fusion.10, bf16[512,896]{0,1:T(8,128)(2,1)S(1)} %bitcast.30, bf16[896,2240]{1,0:T(8,128)(2,1)} %all-gather.3.cloned.1.call-done, bf16[512,2240]{0,1:T(8,128)(2,1)S(1)} %copy-done.2), kind=kOutput, calls=%fused_computation.2 | convolution fusion | flops 2059796480 | bytes 14106624 | tf_op jit(solution)/shard_map/dot_general | solution.py:58
  (3 shorter events, 0.0 us)
Async XLA Ops:
  6.5 49.9 %copy-start = (f32[4,2240]{1,0:T(4,128)S(1)}, f32[4,2240]{1,0:T(4,128)}, u32[]{:S(2)}) copy-start(f32[4,2240]{1,0:T(4,128)} %param.11) | copy-start | bytes 107524
  6.5 7.4 %copy-start.1 = (bf16[2048,224]{0,1:T(8,128)(2,1)S(1)}, bf16[2048,224]{0,1:T(8,128)(2,1)}, u32[]{:S(2)}) copy-start(bf16[2048,224]{0,1:T(8,128)(2,1)} %param.7) | copy-start | bytes 2752516
  6.5 92.0 %all-gather.3.cloned.1.call-start = ((), (), s32[]{:S(2)}) async-start(), calls=%async_computation.1 | async-start | bytes 5160960 | tf_op jit(solution)/shard_map/all_gather | solution.py:60
  52.7 45.9 %copy-start.2 = (bf16[512,2240]{0,1:T(8,128)(2,1)S(1)}, bf16[512,2240]{0,1:T(8,128)(2,1)}, u32[]{:S(2)}) copy-start(bf16[512,2240]{0,1:T(8,128)(2,1)} %param.9) | copy-start | bytes 6881284
  52.7 16.6 %all-to-all-start = ((bf16[4,512,224]{1,2,0:T(8,128)(2,1)}), bf16[4,512,224]{1,2,0:T(8,128)(2,1)S(1)}, u32[]{:S(2)}, u32[]{:S(2)}) async-start(bf16[4,512,224]{1,2,0:T(8,128)(2,1)} %bitcast.5), calls=%async_computation | async-start | bytes 1835008 | tf_op jit(solution)/shard_map/all_to_all | solution.py:57
Sparse Core Ops, SparseCore 0:
  8.9 89.6 all-gather.2
where the time goes:
time: 114 us; the launch traced here: 113 us
  waiting for transfers between devices  38.8 us (34%)
  blocking collectives  33.1 us (29%)
  matrix products  15.5 us (14%)
  between operations  13.5 us (12%)
  local copies, waits for them, and re-layouts  4.76 us (4%)
  other arithmetic  3.95 us (3%)
  starting transfers between devices  3.64 us (3%)
    all_gather x1, waiting for transfers between devices, per_device(): lax.all_gather(out_proj, 'frames', axis=0, tiled=True)  29.2 us
    all_gather x1, blocking collectives, per_device(): lax.all_gather(own_state[None], 'frames', axis=0, tiled=True)  19.9 us
    all_gather x1, blocking collectives, per_device(): lax.all_gather(own_sum[None], 'frames', axis=0, tiled=True)  13.3 us
    all_to_all x1, waiting for transfers between devices, per_device(): lax.all_to_all(attended, 'heads', split_axis=0, concat_axis=1, tiled=True)  8.84 us
    dot_general x1, matrix products, per_device(): jnp.dot(token_rows, lax.all_gather(out_proj, 'frames', axis=0, tiled=True...  7.75 us
    dot_general x1, matrix products, per_device(): jnp.dot(selector, frame_gate, precision=lax.Precision.HIGHEST, preferred_...  4.13 us
    all_to_all x1, starting transfers between devices, per_device(): lax.all_to_all(attended, 'heads', split_axis=0, concat_axis=1, tiled=True)  3.64 us
    reshape x1, local copies, waits for them, and re-layouts, per_device(): value_frames = value_heads.reshape(block_shape)  3.23 us
  transfers between devices with their start and end apart: 2, of which 2 were waited for; matrix products, arithmetic and copies ran while one was open for 14% of the time, Pallas kernels for 0%

commit v1 on v0

--- a/solution.py
+++ b/solution.py
@@ -7,6 +7,28 @@
 HEADS_DEV = 2
 FRAME_TOK = 512
 EPSILON = 1e-06
+
+
+def laid_out(tiles, dim):
+    lengths = list(tiles.shape[1:])
+    lengths[dim] *= tiles.shape[0]
+    return jnp.moveaxis(tiles, 0, dim).reshape(lengths)
+
+
+def grow_blocks(shard, axis):
+    size = lax.axis_size(axis)
+    tiles = shard[None]
+    for level in range(size.bit_length() - 1):
+        bit = 1 << level
+        theirs = lax.ppermute(tiles, axis, [(i, i ^ bit) for i in range(size)])
+        both = jnp.stack([tiles, theirs])
+        upper = lax.axis_index(axis) >> level & 1
+        tiles = jnp.where(upper == 0, both, both[::-1]).reshape(-1, *shard.shape)
+    return tiles
+
+
+def gather_by_bits(x, axis, dim):
+    return laid_out(grow_blocks(x, axis), dim)
 
 
 def per_device(query_heads, key_heads, value_heads, residual, out_proj, frame_gate):
@@ -24,7 +46,7 @@
     own_sum = jnp.sum(frame_sum, axis=0)
     position = lax.axis_index("frames")
     gathered = (
-        lax.all_gather(own_state[None], "frames", axis=0, tiled=True),
+        gather_by_bits(own_state[None], "frames", 0),
         lax.all_gather(own_sum[None], "frames", axis=0, tiled=True),
     )
     pieces = gathered[0].shape[0]

time: 114 us -> 116 us (1.018)
  blocking collectives: 33.1 us -> 10.5 us
  waiting for transfers between devices: 38.8 us -> 59 us
  starting transfers between devices: 3.64 us -> 9.39 us
    ppermute x0 -> x2, waiting for transfers between devices: none -> 23.3 us  [grow_blocks(): theirs = lax.ppermute(tiles, axis, [(i, i ^ bit) for i in range(size)])]
    all_gather x1 -> x0, blocking collectives: 19.9 us -> none  [per_device(): lax.all_gather(own_state[None], 'frames', axis=0, tiled=True)]
    ppermute x0 -> x2, starting transfers between devices: none -> 5.75 us  [grow_blocks(): theirs = lax.ppermute(tiles, axis, [(i, i ^ bit) for i in range(size)])]
    all_gather x1, waiting for transfers between devices: 29.2 us -> 26.1 us  [per_device(): lax.all_gather(out_proj, 'frames', axis=0, tiled=True)]
    all_gather x1, blocking collectives: 13.3 us -> 10.5 us  [per_device(): lax.all_gather(own_sum[None], 'frames', axis=0, tiled=True)]
    max x1, other arithmetic: 1.24 us -> 0.06 us  [per_device(): query_pos = jnp.maximum(query_heads, 0).reshape(block_shape)]
    reduce_sum x1, other arithmetic: 1.44 us -> 0.26 us  [per_device(): own_sum = jnp.sum(frame_sum, axis=0)]
    max x1, other arithmetic: 0.06 us -> 1.24 us  [per_device(): key_pos = jnp.maximum(key_heads, 0).reshape(block_shape)]
  transfers between devices with their start and end apart: 2 -> 4, of which waited for: 2 -> 3; matrix products, arithmetic and copies ran while one was open for 14% -> 13% of each run, Pallas kernels for 0% -> 0%
where the time goes in v1:
time: 116 us
  waiting for transfers between devices  59 us (51%)
  matrix products  15.5 us (13%)
  between operations  13.5 us (12%)
  blocking collectives  10.5 us (9%)
  starting transfers between devices  9.39 us (8%)
  local copies, waits for them, and re-layouts  4.85 us (4%)
  other arithmetic  2.87 us (2%)
    all_gather x1, waiting for transfers between devices, per_device(): lax.all_gather(out_proj, 'frames', axis=0, tiled=True)  26.1 us
    ppermute x2, waiting for transfers between devices, grow_blocks(): theirs = lax.ppermute(tiles, axis, [(i, i ^ bit) for i in range(size)])  23.3 us
    all_gather x1, blocking collectives, per_device(): lax.all_gather(own_sum[None], 'frames', axis=0, tiled=True)  10.5 us
    all_to_all x1, waiting for transfers between devices, per_device(): lax.all_to_all(attended, 'heads', split_axis=0, concat_axis=1, tiled=True)  8.83 us
    dot_general x1, matrix products, per_device(): jnp.dot(token_rows, lax.all_gather(out_proj, 'frames', axis=0, tiled=True...  7.75 us
    ppermute x2, starting transfers between devices, grow_blocks(): theirs = lax.ppermute(tiles, axis, [(i, i ^ bit) for i in range(size)])  5.75 us
    dot_general x1, matrix products, per_device(): jnp.dot(selector, frame_gate, precision=lax.Precision.HIGHEST, preferred_...  4.13 us
    all_to_all x1, starting transfers between devices, per_device(): lax.all_to_all(attended, 'heads', split_axis=0, concat_axis=1, tiled=True)  3.64 us
  transfers between devices with their start and end apart: 4, of which 3 were waited for; matrix products, arithmetic and copies ran while one was open for 13% of the time, Pallas kernels for 0%

profile of v1, /device:TPU:0, one launch (start us, length us, event | category | flops | bytes accessed | tf_op | source)
XLA Modules:
  0.0 115.7 jit_solution(16806402217301887596)
XLA Ops:
  6.5 0.0 copy-start
  6.5 0.0 all-gather.2.cloned.1.call-start
  6.5 0.7 all-gather.2.cloned.1.call-update
  7.3 0.0 copy-start.1
  7.3 3.3 %reshape.52 = bf16[4,512,2,112]{1,0,3,2:T(4,128)(2,1)} reshape(bf16[2048,224]{0,1:T(8,128)(2,1)} %param.8) | data formatting | bytes 1835008 | tf_op jit(solution)/shard_map/reshape | solution.py:40
  10.6 1.2 %broadcast_maximum_fusion.1 = bf16[2048,224]{0,1:T(8,128)(2,1)S(1)} fusion(bf16[2048,224]{0,1:T(8,128)(2,1)} %param.7), kind=kLoop, calls=%fused_computation.20 | loop fusion | flops 458752 | bytes 1835008 | tf_op jit(solution)/shard_map/max | solution.py:39
  11.8 0.7 reshape.51
  12.5 0.0 copy-start.2
  12.5 1.9 %fusion.21 = (f32[2,112,112]{2,1,0:T(8,128)S(1)}, f32[4,2,112,112]{3,2,1,0:T(8,128)S(1)}) fusion(bf16[4,512,2,112]{1,0,3,2:T(4,128)(2,1)} %reshape.52, bf16[4,512,2,112]{1,0,3,2:T(4,128)(2,1)S(1)} %reshape.51), kind=kOutput, calls=%fused_computation.44 | convolution fusion | flops 102835712 | bytes 2336768 | tf_op jit(solution)/shard_map/fthi,fthj->fhij/dot_general | solution.py:41
  14.4 3.1 %collective-permute-start = (f32[1,1,2,112,112]{4,3,2,1,0:T(8,128)S(1)}, f32[1,1,2,112,112]{4,3,2,1,0:T(8,128)S(1)}, u32[]{:S(2)}, u32[]{:S(2)}) collective-permute-start(f32[1,1,2,112,112]{4,3,2,1,0:T(8,128)S(1)} %bitcast.42), channel_id=1, source_target_pairs={{0,4},{4,0},{8,12},{12,8},{1,5},{5,1},{9,13},{13,9},{2,6},{6,2},{1... | collective-permute-start | bytes 301064 | tf_op jit(solution)/shard_map/ppermute | solution.py:23
  17.5 0.0 copy-done.1
  17.5 0.3 convert_reduce_fusion.1
  17.8 0.1 broadcast_in_dim.37
  17.9 0.0 copy-done.2
  17.9 0.1 broadcast_maximum_fusion
  17.9 0.7 reshape.54
  18.6 0.4 convert_reduce_fusion
  19.0 0.4 reduce_window_sum.23
  19.4 10.5 %all_gather.6 = f32[4,2,112]{2,1,0:T(2,128)S(1)} all-gather(f32[1,2,112]{2,1,0:T(2,128)S(1)} %broadcast_in_dim.37), channel_id=1, replica_groups=mesh['groups'=2,'frames'=4,'heads'=4] {'frames'}, dimensions={0}, use_global_device_ids=true | all-gather | bytes 4480 | tf_op jit(solution)/shard_map/all_gather | solution.py:50
  30.0 0.1 select_reduce_fusion
  30.1 0.1 fusion.16
  30.2 0.1 copy.26
  30.3 0.4 fusion.7
  30.7 0.0 collective-permute-done
  30.7 2.6 %collective-permute-start.1 = (f32[2,1,2,112,112]{4,3,2,0,1:T(8,128)S(1)}, f32[2,1,2,112,112]{4,3,2,0,1:T(8,128)S(1)}, u32[]{:S(2)}, u32[]{:S(2)}) collective-permute-start(f32[2,1,2,112,112]{4,3,2,0,1:T(8,128)S(1)} %get-tuple-element.6), channel_id=1, source_target_pairs={{0,8},{4,12},{8,0},{12,4},{1,9},{5,13},{9,1},{13,5},{2,10},{6,14},... | collective-permute-start | bytes 602120 | tf_op jit(solution)/shard_map/ppermute | solution.py:23
  33.4 23.3 %collective-permute-done.1 = f32[2,1,2,112,112]{4,3,2,0,1:T(8,128)S(1)} collective-permute-done((f32[2,1,2,112,112]{4,3,2,0,1:T(8,128)S(1)}, f32[2,1,2,112,112]{4,3,2,0,1:T(8,128)S(1)}, u32[]{:S(2)}, u32[]{:S(2)}) %collective-permute-start.1) | collective-permute-done | bytes 200736 | tf_op jit(solution)/shard_map/ppermute | solution.py:23
  56.7 0.1 fusion.11
  56.9 0.1 fusion.3
  56.9 1.4 %fusion.2 = bf16[4,512,2,112]{1,3,2,0:T(8,128)(2,1)} fusion(bf16[4,2,112,112]{3,2,1,0:T(8,128)(2,1)S(1)} %fusion.3, f32[4,512,2]{1,2,0:T(2,128)S(1)} %fusion.17, bf16[4,512,2,112]{1,0,3,2:T(4,128)(2,1)S(1)} %reshape.54), kind=kOutput, calls=%fused_computation.4 | convolution fusion | flops 103677952 | bytes 2052096 | tf_op jit(solution)/shard_map/fthi,fhij->fthj/dot_general | solution.py:60
  58.3 0.0 copy-start.3
  58.3 3.6 %all-to-all-start = ((bf16[4,512,224]{1,2,0:T(8,128)(2,1)}), bf16[4,512,224]{1,2,0:T(8,128)(2,1)S(1)}, u32[]{:S(2)}, u32[]{:S(2)}) async-start(bf16[4,512,224]{1,2,0:T(8,128)(2,1)} %bitcast.12), calls=%async_computation | async-start | bytes 1835008 | tf_op jit(solution)/shard_map/all_to_all | solution.py:79
  62.0 0.0 copy-done
  62.0 4.1 %fusion.12 = f32[512,2240]{0,1:T(8,128)} fusion(f32[4,2240]{1,0:T(4,128)S(1)} %copy-done, s32[512]{0:T(512)S(1)} %add_select_fusion), kind=kOutput, calls=%fused_computation.23 | convolution fusion | flops 55052288 | bytes 4625408 | tf_op jit(solution)/shard_map/dot_general | solution.py:76
  66.1 8.8 %all-to-all-done = bf16[4,512,224]{1,2,0:T(8,128)(2,1)S(1)} async-done(((bf16[4,512,224]{1,2,0:T(8,128)(2,1)}), bf16[4,512,224]{1,2,0:T(8,128)(2,1)S(1)}, u32[]{:S(2)}, u32[]{:S(2)}) %all-to-all-start) | async-done | bytes 917536 | tf_op jit(solution)/shard_map/all_to_all | solution.py:79
  75.0 26.1 %all-gather.2.cloned.1.call-done = bf16[896,2240]{1,0:T(8,128)(2,1)} async-done(((bf16[224,2240]{1,0:T(8,128)(2,1)}), bf16[896,2240]{1,0:T(8,128)(2,1)}) %all-gather.2.cloned.1.call-update) | async-done | bytes 4014096 | tf_op jit(solution)/shard_map/all_gather | solution.py:82
  101.1 0.0 copy-done.3
  101.1 7.8 %fusion.1 = bf16[512,2240]{0,1:T(8,128)(2,1)} fusion(f32[512,2240]{0,1:T(8,128)} %fusion.12, bf16[512,896]{0,1:T(8,128)(2,1)S(1)} %bitcast.40, bf16[896,2240]{1,0:T(8,128)(2,1)} %all-gather.2.cloned.1.call-done, bf16[512,2240]{0,1:T(8,128)(2,1)S(1)} %copy-done.3), kind=kOutput, calls=%fused_computation.2 | convolution fusion | flops 2059796480 | bytes 14106624 | tf_op jit(solution)/shard_map/dot_general | solution.py:80
  (7 shorter events, 0.1 us)
Async XLA Ops:
  6.5 55.5 %copy-start = (f32[4,2240]{1,0:T(4,128)S(1)}, f32[4,2240]{1,0:T(4,128)}, u32[]{:S(2)}) copy-start(f32[4,2240]{1,0:T(4,128)} %param.11) | copy-start | bytes 107524
  6.5 94.5 %all-gather.2.cloned.1.call-start = ((), (), s32[]{:S(2)}) async-start(), calls=%async_computation.1 | async-start | bytes 5160960 | tf_op jit(solution)/shard_map/all_gather | solution.py:82
  7.3 10.3 %copy-start.1 = (bf16[2048,224]{0,1:T(8,128)(2,1)S(1)}, bf16[2048,224]{0,1:T(8,128)(2,1)}, u32[]{:S(2)}) copy-start(bf16[2048,224]{0,1:T(8,128)(2,1)} %param.7) | copy-start | bytes 2752516
  12.5 5.4 %copy-start.2 = (bf16[2048,224]{0,1:T(8,128)(2,1)S(1)}, bf16[2048,224]{0,1:T(8,128)(2,1)}, u32[]{:S(2)}) copy-start(bf16[2048,224]{0,1:T(8,128)(2,1)} %param.6) | copy-start | bytes 2752516
  14.4 16.3 %collective-permute-start = (f32[1,1,2,112,112]{4,3,2,1,0:T(8,128)S(1)}, f32[1,1,2,112,112]{4,3,2,1,0:T(8,128)S(1)}, u32[]{:S(2)}, u32[]{:S(2)}) collective-permute-start(f32[1,1,2,112,112]{4,3,2,1,0:T(8,128)S(1)} %bitcast.42), channel_id=1, source_target_pairs={{0,4},{4,0},{8,12},{12,8},{1,5},{5,1},{9,13},{13,9},{2,6},{6,2},{1... | collective-permute-start | bytes 301064 | tf_op jit(solution)/shard_map/ppermute | solution.py:23
  30.7 26.0 %collective-permute-start.1 = (f32[2,1,2,112,112]{4,3,2,0,1:T(8,128)S(1)}, f32[2,1,2,112,112]{4,3,2,0,1:T(8,128)S(1)}, u32[]{:S(2)}, u32[]{:S(2)}) collective-permute-start(f32[2,1,2,112,112]{4,3,2,0,1:T(8,128)S(1)} %get-tuple-element.6), channel_id=1, source_target_pairs={{0,8},{4,12},{8,0},{12,4},{1,9},{5,13},{9,1},{13,5},{2,10},{6,14},... | collective-permute-start | bytes 602120 | tf_op jit(solution)/shard_map/ppermute | solution.py:23
  58.3 42.8 %copy-start.3 = (bf16[512,2240]{0,1:T(8,128)(2,1)S(1)}, bf16[512,2240]{0,1:T(8,128)(2,1)}, u32[]{:S(2)}) copy-start(bf16[512,2240]{0,1:T(8,128)(2,1)} %param.9) | copy-start | bytes 6881284
  58.3 16.6 %all-to-all-start = ((bf16[4,512,224]{1,2,0:T(8,128)(2,1)}), bf16[4,512,224]{1,2,0:T(8,128)(2,1)S(1)}, u32[]{:S(2)}, u32[]{:S(2)}) async-start(bf16[4,512,224]{1,2,0:T(8,128)(2,1)} %bitcast.12), calls=%async_computation | async-start | bytes 1835008 | tf_op jit(solution)/shard_map/all_to_all | solution.py:79
Sparse Core Ops, SparseCore 0:
  8.9 92.1 all-gather.1
